TPU v7x, 256 devices: a whole 4x4x8 slice. The times are simulated.
256 devices in a mesh: dp: 32 (over y, z), mp: 8 (over x, core).
Axes of the slice: x: 4, y: 4, z: 8, core: 2. Of those that a mesh axis runs over, the one named last changes fastest.
Arguments:
- hidden: bfloat16 [512, 32, 1024], P(('dp', 'mp')), may hold values from -96 to 96, as said below
- query_weight: bfloat16 [1024, 1024], P('dp', 'mp'), may hold values from -0.1875 to 0.1875
- w_key: bfloat16 [1024, 1024], P('dp', 'mp'), may hold values from -0.1875 to 0.1875
- w_value: bfloat16 [1024, 1024], P('dp', 'mp'), may hold values from -0.1875 to 0.1875
- rel_table: bfloat16 [512, 1024], P('dp'), may hold values from -6 to 6
- rel_bucket: int32 [32, 32], replicated, may hold values from 0 to 511
- w_out: bfloat16 [1024, 1024], P('mp', 'dp'), may hold values from -0.1875 to 0.1875
- w_up: bfloat16 [1024, 4096], P('dp', 'mp'), may hold values from -0.1875 to 0.1875
- w_down: bfloat16 [4096, 1024], P('mp', 'dp'), may hold values from -0.09375 to 0.09375
- w_proj: bfloat16 [1024, 128], P(('dp', 'mp')), may hold values from -0.1875 to 0.1875
- pages: bfloat16 [8192, 128, 128], P('dp'), may hold values from -0.59765625 to 0.59765625
- page_len: int32 [8192], P('dp'), may hold values from 1 to 128
- slot_per_page: int32 [8192], replicated, may hold values from 0 to 8191, as said below
- candidates: int32 [512, 16, 4], P(('dp', 'mp')), may hold values from 0 to 8191, as said below
Outputs:
- query_vectors: bfloat16 [512, 32, 128], P(('dp', 'mp'))
- scores: float32 [512, 16], P(('dp', 'mp'))
Inputs may be any that keep to these rules, and one draw needn't show every extreme that they name: slot_per_page is a permutation of the slots; the page in slot s is held by index s // 256 of dp. `candidates`: among the 128 page ids of the 2 queries of one device (queries in aligned blocks of 2), at most 8 have slots held by any one index of dp, and in every such block some index of dp holds exactly 8 of them. `hidden`: token states are finite.
All inputs are finite; a program needn't handle non-finite values.
Results may differ from a plain program's by a relative error of at most 0.025.
Values may be sent and summed in bfloat16 or wider, within the bound.
No kernel may reach another device: no remote copies, remote signals or barrier semaphores. Data moves between devices by JAX's collectives and lax.ppermute only.
A program may use at most 64 MiB of HBM per device.

v0:
```python
import jax
import jax.numpy as jnp
from jax import lax
from jax.sharding import PartitionSpec as P

HD = 64


def layer_norm(value):
    mean = jnp.mean(value, axis=-1, keepdims=True)
    centered = value - mean
    var = jnp.mean(centered * centered, axis=-1, keepdims=True)
    return centered / jnp.sqrt(var + 1e-07)


def add_rows(left, piece):
    return jnp.dot(left, piece, preferred_element_type=jnp.float32)


def return_maxima(maxima):
    return lax.all_to_all(
        maxima.astype(jnp.bfloat16), "dp", split_axis=0, concat_axis=0, tiled=True
    ).astype(maxima.dtype)


def body(
    hidden,
    query_weight,
    w_key,
    w_value,
    rel_table,
    rel_bucket,
    w_out,
    w_up,
    w_down,
    w_proj,
    pages,
    page_len,
    slot_per_page,
    candidates,
):
    qry_dev, qlen, width = hidden.shape
    heads_local = query_weight.shape[1] // HD
    cols = query_weight.shape[1]
    tokens = lax.all_gather(hidden, "mp", axis=0, tiled=True)
    group = tokens.shape[0]
    flat = tokens.reshape(group * qlen, width)
    left_rel = lax.all_gather(rel_table, "dp", axis=0, tiled=True)
    pieces = (
        lax.all_gather(query_weight, "dp", axis=0, tiled=True),
        lax.all_gather(w_key, "dp", axis=0, tiled=True),
        lax.all_gather(w_value, "dp", axis=0, tiled=True),
    )
    qsum = add_rows(flat, pieces[0])
    ksum = add_rows(flat, pieces[1])
    vsum = add_rows(flat, pieces[2])
    qrsum = add_rows(left_rel, pieces[0])
    krsum = add_rows(left_rel, pieces[1])
    rel_q = qrsum.astype(jnp.bfloat16)
    rel_k = krsum.astype(jnp.bfloat16)
    nbuck = rel_q.shape[0]
    qx = qsum.astype(jnp.bfloat16).reshape(group, qlen, heads_local, HD)
    kx = ksum.astype(jnp.bfloat16).reshape(group, qlen, heads_local, HD)
    vx = vsum.astype(jnp.bfloat16).reshape(group, qlen, heads_local, HD)
    rel_q = rel_q.reshape(nbuck, heads_local, HD)
    rel_k = rel_k.reshape(nbuck, heads_local, HD)
    onehot = (rel_bucket[:, :, None] == jnp.arange(nbuck, dtype=jnp.int32)[None, None, :]).astype(
        jnp.float32
    )
    scale = 1.0 / jnp.sqrt(jnp.float32(3 * HD))
    content = jnp.einsum("qihd,qjhd->qhij", qx, kx, preferred_element_type=jnp.float32)
    along_axis_name = jnp.einsum("qihd,bhd->qhib", qx, rel_k, preferred_element_type=jnp.float32)
    c2p = jnp.einsum("qhib,ijb->qhij", along_axis_name, onehot, precision=lax.Precision.HIGHEST)
    back = jnp.einsum("qjhd,bhd->qhjb", kx, rel_q, preferred_element_type=jnp.float32)
    p2c = jnp.einsum("qhjb,jib->qhij", back, onehot, precision=lax.Precision.HIGHEST)
    logits = (content + c2p + p2c) * scale
    probs = jax.nn.softmax(logits, axis=-1).astype(jnp.bfloat16)
    context_rows = jnp.einsum("qhij,qjhd->qihd", probs, vx, preferred_element_type=jnp.float32)
    context_rows = context_rows.astype(jnp.bfloat16).reshape(group * qlen, cols)
    attn_terms = jnp.dot(
        context_rows,
        lax.all_gather(w_out, "dp", axis=1, tiled=True),
        preferred_element_type=jnp.float32,
    )
    attn = lax.psum_scatter(
        attn_terms.astype(jnp.bfloat16), "mp", scatter_dimension=0, tiled=True
    ).astype(jnp.float32)
    own = hidden.reshape(qry_dev * qlen, width).astype(jnp.float32)
    mid = layer_norm(own + attn).astype(jnp.bfloat16)
    mid_all = lax.all_gather(mid, "mp", axis=0, tiled=True)
    up = add_rows(mid_all, lax.all_gather(w_up, "dp", axis=0, tiled=True))
    inner = jax.nn.gelu(up, approximate=False).astype(jnp.bfloat16)
    down_terms = jnp.dot(
        inner, lax.all_gather(w_down, "dp", axis=1, tiled=True), preferred_element_type=jnp.float32
    )
    mlp = lax.psum_scatter(
        down_terms.astype(jnp.bfloat16), "mp", scatter_dimension=0, tiled=True
    ).astype(jnp.float32)
    state = layer_norm(mid.astype(jnp.float32) + mlp).astype(jnp.bfloat16)
    width_out = w_proj.shape[1]
    proj = add_rows(state, lax.all_gather(w_proj, ("dp", "mp"), axis=0, tiled=True))
    vectors = (proj / jnp.sqrt(jnp.sum(proj * proj, axis=-1, keepdims=True) + 1e-06)).astype(
        jnp.bfloat16
    )
    vectors = vectors.reshape(qry_dev, qlen, width_out)
    page_owners = lax.axis_size("dp")
    pg_dev = pages.shape[0]
    ptok = pages.shape[1]
    ncand, ppc = (candidates.shape[1], candidates.shape[2])
    req = qry_dev * ncand * ppc
    cap = 2 * req // page_owners
    slots = slot_per_page[candidates.reshape(req)]
    dest = slots // pg_dev
    local = slots % pg_dev
    query_of = jnp.arange(req, dtype=jnp.int32) // (ncand * ppc)
    member = (dest[:, None] == jnp.arange(page_owners, dtype=jnp.int32)[None, :]).astype(jnp.int32)
    place = jnp.sum((jnp.cumsum(member, axis=0) - 1) * member, axis=1)
    index = dest * cap + place
    codes = jnp.full((page_owners * cap,), -1, jnp.int32).at[index].set(query_of * pg_dev + local)
    codes = codes.reshape(page_owners, cap)
    token_positions = jnp.arange(ptok, dtype=jnp.int32)
    rows_out = (
        jnp.zeros((page_owners * cap, qlen, width_out), jnp.bfloat16)
        .at[index]
        .set(vectors[query_of])
    )
    rows_out = rows_out.reshape(page_owners, cap, qlen, width_out)
    where_local = lax.all_to_all(codes, "dp", split_axis=0, concat_axis=0, tiled=True) % pg_dev
    chosen = pages[where_local]
    lens = page_len[where_local]
    sim = jnp.einsum(
        "snie,snte->snit",
        lax.all_to_all(rows_out, "dp", split_axis=0, concat_axis=0, tiled=True),
        chosen,
        preferred_element_type=jnp.float32,
    )
    valid = token_positions[None, None, None, :] < lens[:, :, None, None]
    returned = return_maxima(jnp.max(jnp.where(valid, sim, -1e30), axis=-1))
    best = returned.reshape(page_owners * cap, qlen)[index]
    best = best.reshape(qry_dev, ncand, ppc, qlen)
    scores = jnp.sum(jnp.max(best, axis=2), axis=-1)
    return (vectors, scores)


def solution(mesh):
    in_specs = (
        P(("dp", "mp"), None, None),
        P("dp", "mp"),
        P("dp", "mp"),
        P("dp", "mp"),
        P("dp", None),
        P(),
        P("mp", "dp"),
        P("dp", "mp"),
        P("mp", "dp"),
        P(("dp", "mp"), None),
        P("dp", None, None),
        P("dp"),
        P(),
        P(("dp", "mp"), None, None),
    )
    out_specs = (P(("dp", "mp"), None, None), P(("dp", "mp"), None))
    return jax.shard_map(body, mesh=mesh, in_specs=in_specs, out_specs=out_specs, check_vma=False)
```

profile of v0, /device:TPU:1, one launch (start us, length us, event | category | flops | bytes accessed | tf_op | source)
XLA Modules:
  0.0 620.8 jit_solution(7747046523202727993)
XLA Ops:
  8.7 41.4 %all_gather.32 = bf16[1024,128]{1,0:T(8,128)(2,1)S(1)} all-gather(bf16[32,128]{1,0:T(8,128)(2,1)} %param.15), channel_id=1, replica_groups=mesh['dp'=32,'mp'=8] {'dp'}, dimensions={0}, use_global_device_ids=true | all-gather | bytes 270336 | tf_op jit(solution)/shard_map/all_gather | solution.py:50
  50.1 38.1 %all_gather.33 = bf16[1024,128]{1,0:T(8,128)(2,1)S(1)} all-gather(bf16[32,128]{1,0:T(8,128)(2,1)} %param.16), channel_id=1, replica_groups=mesh['dp'=32,'mp'=8] {'dp'}, dimensions={0}, use_global_device_ids=true | all-gather | bytes 270336 | tf_op jit(solution)/shard_map/all_gather | solution.py:51
  88.1 37.2 %all_gather.31 = bf16[1024,128]{1,0:T(8,128)(2,1)S(1)} all-gather(bf16[32,128]{1,0:T(8,128)(2,1)} %param.17), channel_id=1, replica_groups=mesh['dp'=32,'mp'=8] {'dp'}, dimensions={0}, use_global_device_ids=true | all-gather | bytes 270336 | tf_op jit(solution)/shard_map/all_gather | solution.py:52
  125.3 35.7 %all_gather.35 = bf16[128,1024]{0,1:T(8,128)(2,1)S(1)} all-gather(bf16[128,32]{0,1:T(8,128)(2,1)} %param.20), channel_id=1, replica_groups=mesh['dp'=32,'mp'=8] {'dp'}, dimensions={1}, use_global_device_ids=true | all-gather | bytes 270336 | tf_op jit(solution)/shard_map/all_gather | solution.py:82
  161.0 1.7 convolution_convert_fusion.6
  162.9 1.7 convolution_convert_fusion.5
  165.3 1.7 convolution_convert_fusion.4
  167.6 1.4 fusion.3
  170.2 1.4 fusion.1
  173.0 1.4 convolution_convert_fusion
  175.7 73.5 %reduce-scatter.3.cloned.1.call-done = bf16[64,1024]{1,0:T(8,128)(2,1)} async-done(((bf16[512,1024]{1,0:T(8,128)(2,1)}), bf16[64,1024]{1,0:T(8,128)(2,1)}) %reduce-scatter.3.cloned.1.call-update) | async-done | bytes 131088 | tf_op jit(solution)/shard_map/reduce_scatter | solution.py:85
  249.2 1.0 fusion.67
  250.3 1.1 multiply_reduce_fusion.1
  251.4 1.7 divide_convert_fusion.3
  253.4 70.8 %all-gather.13.cloned.1.call-done = bf16[1024,512]{1,0:T(8,128)(2,1)} async-done(((bf16[32,512]{1,0:T(8,128)(2,1)}), bf16[1024,512]{1,0:T(8,128)(2,1)}) %all-gather.13.cloned.1.call-update) | async-done | bytes 1048592 | tf_op jit(solution)/shard_map/all_gather | solution.py:91
  324.1 76.3 %all-gather.15.cloned.1.call-done = bf16[512,1024]{0,1:T(8,128)(2,1)} async-done(((bf16[512,32]{0,1:T(8,128)(2,1)}), bf16[512,1024]{0,1:T(8,128)(2,1)}) %all-gather.15.cloned.1.call-update) | async-done | bytes 1048592 | tf_op jit(solution)/shard_map/all_gather | solution.py:94
  400.4 30.5 %all-gather.11.cloned.1.call-done = bf16[512,1024]{1,0:T(8,128)(2,1)} async-done(((bf16[64,1024]{1,0:T(8,128)(2,1)}), bf16[512,1024]{1,0:T(8,128)(2,1)}) %all-gather.11.cloned.1.call-update) | async-done | bytes 1048592 | tf_op jit(solution)/shard_map/all_gather | solution.py:90
  430.9 6.2 %convolution_convert_fusion.1 = bf16[512,1024]{1,0:T(8,128)(2,1)} fusion(bf16[512,1024]{0,1:T(8,128)(2,1)} %all-gather.15.cloned.1.call-done, bf16[512,1024]{1,0:T(8,128)(2,1)} %all-gather.11.cloned.1.call-done, bf16[1024,512]{1,0:T(8,128)(2,1)} %all-gather.13.cloned.1.call-done), kind=kOutput, calls=%fused_computation.17 | convolution fusion | flops 1091305472 | bytes 4194304 | tf_op jit(solution)/shard_map/dot_general | solution.py:93
  437.4 1.1 gather_fusion
  440.7 9.6 %all-to-all-start = ((s32[32,1,8]{2,1,0:T(1,128)}), s32[32,1,8]{2,1,0:T(1,128)S(1)}, u32[]{:S(2)}, u32[]{:S(2)}) async-start(s32[32,1,8]{2,1,0:T(1,128)} %bitcast.21), calls=%async_computation.2 | async-start | bytes 32768 | tf_op jit(solution)/shard_map/all_to_all | solution.py:128
  450.3 62.5 %all-gather = bf16[256,4,128]{2,1,0:T(4,128)(2,1)S(1)} all-gather(bf16[1,4,128]{2,1,0:T(4,128)(2,1)S(1)} %bitcast.96), channel_id=1, replica_groups=mesh['dp'=32,'mp'=8] {'dp','mp'}, dimensions={0}, use_global_device_ids=true | all-gather | bytes 263168 | tf_op jit(solution)/shard_map/all_gather | solution.py:101
  513.9 1.1 multiply_reduce_fusion
  515.0 1.3 multiply_reduce_fusion.2
  517.2 1.7 broadcast_in_dim.14
  518.8 13.7 %scatter_fusion = bf16[256,32,128]{2,1,0:T(8,128)(2,1)} fusion(bf16[256,32,128]{2,1,0:T(8,128)(2,1)} %broadcast_in_dim.14, s32[128]{0:T(128)S(1)} %fusion.75, bf16[128,32,128]{2,1,0:T(8,128)(2,1)S(1)} %gather_fusion.2), kind=kCustom, calls=%fused_computation.6 | custom fusion | bytes 3146240 | tf_op jit(solution)/shard_map/scatter | solution.py:125
  532.5 6.3 %all-to-all-start.1 = ((bf16[32,8,32,128]{3,2,1,0:T(8,128)(2,1)}), bf16[32,8,32,128]{3,2,1,0:T(8,128)(2,1)S(1)}, u32[]{:S(2)}, u32[]{:S(2)}) async-start(bf16[32,8,32,128]{3,2,1,0:T(8,128)(2,1)} %bitcast.24), calls=%async_computation.3 | async-start | bytes 4194304 | tf_op jit(solution)/shard_map/all_to_all | solution.py:133
  538.9 11.8 %gather_fusion.3 = bf16[256,128,128]{2,1,0:T(8,128)(2,1)} fusion(bf16[256,128,128]{2,1,0:T(8,128)(2,1)} %param.24, s32[1024]{0:T(1024)S(1)} %pad_clamp_fusion.2), kind=kCustom, calls=%fused_computation.3 | custom fusion | bytes 16778240 | tf_op jit(solution)/shard_map/gather | solution.py:129
  550.8 1.9 gather_fusion.1
  552.9 34.5 %all-to-all-done.1 = bf16[32,8,32,128]{3,2,1,0:T(8,128)(2,1)S(1)} async-done(((bf16[32,8,32,128]{3,2,1,0:T(8,128)(2,1)}), bf16[32,8,32,128]{3,2,1,0:T(8,128)(2,1)S(1)}, u32[]{:S(2)}, u32[]{:S(2)}) %all-to-all-start.1) | async-done | bytes 2097184 | tf_op jit(solution)/shard_map/all_to_all | solution.py:133
  587.4 8.0 %select_reduce_fusion = bf16[32,8,32]{2,1,0:T(8,128)(2,1)S(1)} fusion(bf16[32,8,32,128]{3,2,1,0:T(8,128)(2,1)S(1)} %all-to-all-done.1, bf16[32,8,128,128]{3,2,1,0:T(8,128)(2,1)} %bitcast.87, pred[32,8,128]{2,1,0:T(8,128)(4,1)S(1)} %iota_compare_fusion.1), kind=kOutput, calls=%fused_computation.8 | convolution fusion | flops 270524416 | bytes 10534912 | tf_op jit(solution)/shard_map/snie,snte->snit/dot_general | solution.py:131
  596.0 7.8 %all-to-all-start.2 = ((bf16[32,2,128]{2,1,0:T(2,128)(2,1)}), bf16[32,2,128]{2,1,0:T(2,128)(2,1)S(1)}, u32[]{:S(2)}, u32[]{:S(2)}) async-start(bf16[32,2,128]{2,1,0:T(2,128)(2,1)} %reshape.374), calls=%async_computation.4 | async-start | bytes 32768 | tf_op jit(solution)/shard_map/all_to_all | solution.py:21
  603.8 8.6 %all-to-all-done.2 = bf16[32,2,128]{2,1,0:T(2,128)(2,1)S(1)} async-done(((bf16[32,2,128]{2,1,0:T(2,128)(2,1)}), bf16[32,2,128]{2,1,0:T(2,128)(2,1)S(1)}, u32[]{:S(2)}, u32[]{:S(2)}) %all-to-all-start.2) | async-done | bytes 16416 | tf_op jit(solution)/shard_map/all_to_all | solution.py:21
  (84 shorter events, 13.7 us)
Async XLA Ops:
  7.2 430.2 %copy-start = (s32[8192]{0:T(1024)S(1)}, s32[8192]{0:T(1024)}, u32[]{:S(2)}) copy-start(s32[8192]{0:T(1024)} %param.26) | copy-start | bytes 98308
  7.2 153.8 %all-gather.7.cloned.1.call-start = ((), (), s32[]{:S(2)}) async-start(), calls=%async_computation.5 | async-start | bytes 1179648 | tf_op jit(solution)/shard_map/all_gather | solution.py:45
  7.9 157.4 %all-gather.9.cloned.1.call-start = ((), (), s32[]{:S(2)}) async-start(), calls=%async_computation.6 | async-start | bytes 1081344 | tf_op jit(solution)/shard_map/all_gather | solution.py:48
  8.7 240.6 %reduce-scatter.3.cloned.1.call-start = ((), (), s32[]{:S(2)}) async-start(), calls=%async_computation.7 | async-start | bytes 1179648 | tf_op jit(solution)/shard_map/reduce_scatter | solution.py:85
  161.0 3.7 copy-start.3
  165.2 2.4 copy-start.7
  167.5 1.7 copy-start.4
  172.6 76.6 %copy-start.5 = (bf16[2,32,1024]{2,1,0:T(8,128)(2,1)S(1)}, bf16[2,32,1024]{2,1,0:T(8,128)(2,1)}, u32[]{:S(2)}) copy-start(bf16[2,32,1024]{2,1,0:T(8,128)(2,1)} %param.14) | copy-start | bytes 393220
  174.5 149.6 %all-gather.13.cloned.1.call-start = ((), (), s32[]{:S(2)}) async-start(), calls=%async_computation.9 | async-start | bytes 1081344 | tf_op jit(solution)/shard_map/all_gather | solution.py:91
  175.1 225.4 %all-gather.15.cloned.1.call-start = ((), (), s32[]{:S(2)}) async-start(), calls=%async_computation.10 | async-start | bytes 1081344 | tf_op jit(solution)/shard_map/all_gather | solution.py:94
  175.7 255.2 %all-gather.11.cloned.1.call-start = ((), (), s32[]{:S(2)}) async-start(), calls=%async_computation.8 | async-start | bytes 1179648 | tf_op jit(solution)/shard_map/all_gather | solution.py:90
  253.1 184.0 %copy-start.8 = (s32[2,16,4]{1,2,0:T(4,128)S(1)}, s32[2,16,4]{1,2,0:T(4,128)}, u32[]{:S(2)}) copy-start(s32[2,16,4]{1,2,0:T(4,128)} %param.27) | copy-start | bytes 1540
  253.1 197.2 %copy-start.9 = (bf16[4,128]{1,0:T(4,128)(2,1)S(1)}, bf16[4,128]{1,0:T(4,128)(2,1)}, u32[]{:S(2)}) copy-start(bf16[4,128]{1,0:T(4,128)(2,1)} %param.23) | copy-start | bytes 3076
  253.1 259.7 %reduce-scatter.5.cloned.1.call-start = ((), (), s32[]{:S(2)}) async-start(), calls=%async_computation.11 | async-start | bytes 1179648 | tf_op jit(solution)/shard_map/reduce_scatter | solution.py:96
  437.1 75.7 %copy-start.6 = (bf16[64,1024]{1,0:T(8,128)(2,1)S(1)}, bf16[64,1024]{1,0:T(8,128)(2,1)}, u32[]{:S(2)}) copy-start(bf16[64,1024]{1,0:T(8,128)(2,1)} %divide_convert_fusion.3) | copy-start | bytes 393220
  440.7 91.9 %all-to-all-start = ((s32[32,1,8]{2,1,0:T(1,128)}), s32[32,1,8]{2,1,0:T(1,128)S(1)}, u32[]{:S(2)}, u32[]{:S(2)}) async-start(s32[32,1,8]{2,1,0:T(1,128)} %bitcast.21), calls=%async_computation.2 | async-start | bytes 32768 | tf_op jit(solution)/shard_map/all_to_all | solution.py:128
  516.4 2.5 copy-start.2
  532.5 54.9 %all-to-all-start.1 = ((bf16[32,8,32,128]{3,2,1,0:T(8,128)(2,1)}), bf16[32,8,32,128]{3,2,1,0:T(8,128)(2,1)S(1)}, u32[]{:S(2)}, u32[]{:S(2)}) async-start(bf16[32,8,32,128]{3,2,1,0:T(8,128)(2,1)} %bitcast.24), calls=%async_computation.3 | async-start | bytes 4194304 | tf_op jit(solution)/shard_map/all_to_all | solution.py:133
  538.9 11.8 %copy-start.1 = (s32[256]{0:T(256)S(1)}, s32[256]{0:T(256)}, u32[]{:S(2)}) copy-start(s32[256]{0:T(256)} %param.25) | copy-start | bytes 3076
  596.0 16.4 %all-to-all-start.2 = ((bf16[32,2,128]{2,1,0:T(2,128)(2,1)}), bf16[32,2,128]{2,1,0:T(2,128)(2,1)S(1)}, u32[]{:S(2)}, u32[]{:S(2)}) async-start(bf16[32,2,128]{2,1,0:T(2,128)(2,1)} %reshape.374), calls=%async_computation.4 | async-start | bytes 32768 | tf_op jit(solution)/shard_map/all_to_all | solution.py:21
Sparse Core Ops, SparseCore 0:
  9.8 29.9 all-gather.6
  42.4 71.3 all-gather.8
  174.6 74.5 reduce-scatter.2
  251.7 72.3 all-gather.12
  326.6 73.8 all-gather.14
  402.1 28.6 all-gather.10
  437.2 32.1 reduce-scatter.4
where the time goes:
time: 622 us; the launch traced here: 621 us
  waiting for transfers between devices  297 us (48%)
  blocking collectives  215 us (35%)
  local copies, waits for them, and re-layouts  35.7 us (6%)
  matrix products  27.4 us (4%)
  starting transfers between devices  24 us (4%)
  between operations  14.6 us (2%)
  other arithmetic  7.57 us (1%)
    all_gather x1, waiting for transfers between devices, body(): lax.all_gather(w_down, 'dp', axis=1, tiled=True)  76.3 us
    reduce_scatter x1, waiting for transfers between devices, body(): lax.psum_scatter(attn_terms.astype(jnp.bfloat16), 'mp', scatter_dimension...  73.5 us
    all_gather x1, waiting for transfers between devices, body(): up = add_rows(mid_all, lax.all_gather(w_up, 'dp', axis=0, tiled=True))  70.8 us
    all_gather x1, blocking collectives, body(): lax.all_gather(w_proj, ('dp', 'mp'), axis=0, tiled=True)  62.5 us
    all_gather x1, blocking collectives, body(): lax.all_gather(query_weight, 'dp', axis=0, tiled=True)  41.4 us
    all_gather x1, blocking collectives, body(): lax.all_gather(w_key, 'dp', axis=0, tiled=True)  38.1 us
    all_gather x1, blocking collectives, body(): lax.all_gather(w_value, 'dp', axis=0, tiled=True)  37.2 us
    all_gather x1, blocking collectives, body(): lax.all_gather(w_out, 'dp', axis=1, tiled=True)  35.7 us
  transfers between devices with their start and end apart: 10, of which 6 were waited for; matrix products, arithmetic and copies ran while one was open for 7% of the time, Pallas kernels for 0%

commit v1 on v0

--- a/solution.py
+++ b/solution.py
@@ -4,6 +4,13 @@
 from jax.sharding import PartitionSpec as P
 
 HD = 64
+
+
+def all_by_exchange(x, axis, dim):
+    count = lax.axis_size(axis)
+    blocks = jnp.stack([x for _ in range(count)])
+    blocks = lax.all_to_all(blocks, axis, split_axis=0, concat_axis=0)
+    return jnp.concatenate(blocks, axis=dim)
 
 
 def layer_norm(value):
@@ -48,7 +55,7 @@
     left_rel = lax.all_gather(rel_table, "dp", axis=0, tiled=True)
     pieces = (
         lax.all_gather(query_weight, "dp", axis=0, tiled=True),
-        lax.all_gather(w_key, "dp", axis=0, tiled=True),
+        all_by_exchange(w_key, "dp", 0),
         lax.all_gather(w_value, "dp", axis=0, tiled=True),
     )
     qsum = add_rows(flat, pieces[0])

time: 622 us -> 588 us (0.945)
  blocking collectives: 215 us -> 177 us
  starting transfers between devices: 24 us -> 36.1 us
  waiting for transfers between devices: 297 us -> 286 us
    all_gather x1 -> x0, blocking collectives: 38.1 us -> none  [body(): lax.all_gather(w_key, 'dp', axis=0, tiled=True)]
    all_to_all x0 -> x1, starting transfers between devices: none -> 12 us  [all_by_exchange(): blocks = lax.all_to_all(blocks, axis, split_axis=0, concat_axis=0)]
    reduce_scatter x1, waiting for transfers between devices: 73.5 us -> 62.7 us  [body(): lax.psum_scatter(attn_terms.astype(jnp.bfloat16), 'mp', scatter_dimension...]
  transfers between devices with their start and end apart: 10 -> 11, of which waited for: 6 -> 6; matrix products, arithmetic and copies ran while one was open for 7% -> 8% of each run, Pallas kernels for 0% -> 0%
where the time goes in v1:
time: 588 us; the launch traced here: 586 us
  waiting for transfers between devices  286 us (49%)
  blocking collectives  177 us (30%)
  local copies, waits for them, and re-layouts  37.9 us (6%)
  starting transfers between devices  36.1 us (6%)
  matrix products  27.4 us (5%)
  between operations  14.6 us (2%)
  other arithmetic  7.57 us (1%)
    all_gather x1, waiting for transfers between devices, body(): lax.all_gather(w_down, 'dp', axis=1, tiled=True)  76.3 us
    all_gather x1, waiting for transfers between devices, body(): up = add_rows(mid_all, lax.all_gather(w_up, 'dp', axis=0, tiled=True))  70.8 us
    reduce_scatter x1, waiting for transfers between devices, body(): lax.psum_scatter(attn_terms.astype(jnp.bfloat16), 'mp', scatter_dimension...  62.7 us
    all_gather x1, blocking collectives, body(): lax.all_gather(w_proj, ('dp', 'mp'), axis=0, tiled=True)  62.5 us
    all_gather x1, blocking collectives, body(): lax.all_gather(query_weight, 'dp', axis=0, tiled=True)  39.9 us
    all_gather x1, blocking collectives, body(): lax.all_gather(w_value, 'dp', axis=0, tiled=True)  38.7 us
    all_gather x1, blocking collectives, body(): lax.all_gather(w_out, 'dp', axis=1, tiled=True)  35.8 us
    all_to_all x1, waiting for transfers between devices, body(): lax.all_to_all(rows_out, 'dp', split_axis=0, concat_axis=0, tiled=True)  34.5 us
  transfers between devices with their start and end apart: 11, of which 6 were waited for; matrix products, arithmetic and copies ran while one was open for 8% of the time, Pallas kernels for 0%

profile of v1, /device:TPU:1, one launch (start us, length us, event | category | flops | bytes accessed | tf_op | source)
XLA Modules:
  0.0 586.3 jit_solution(3445798962036728554)
XLA Ops:
  8.7 1.5 stack.2
  10.1 12.0 %all-to-all-start = ((bf16[32,32,128]{2,1,0:T(8,128)(2,1)}), bf16[32,32,128]{2,1,0:T(8,128)(2,1)S(1)}, u32[]{:S(2)}, u32[]{:S(2)}) async-start(bf16[32,32,128]{2,1,0:T(8,128)(2,1)} %stack.2), calls=%async_computation | async-start | bytes 524288 | tf_op jit(solution)/shard_map/all_to_all | solution.py:12
  22.2 39.9 %all_gather.29 = bf16[1024,128]{1,0:T(8,128)(2,1)S(1)} all-gather(bf16[32,128]{1,0:T(8,128)(2,1)} %param.15), channel_id=1, replica_groups=mesh['dp'=32,'mp'=8] {'dp'}, dimensions={0}, use_global_device_ids=true | all-gather | bytes 270336 | tf_op jit(solution)/shard_map/all_gather | solution.py:57
  62.1 38.7 %all_gather.28 = bf16[1024,128]{1,0:T(8,128)(2,1)S(1)} all-gather(bf16[32,128]{1,0:T(8,128)(2,1)} %param.17), channel_id=1, replica_groups=mesh['dp'=32,'mp'=8] {'dp'}, dimensions={0}, use_global_device_ids=true | all-gather | bytes 270336 | tf_op jit(solution)/shard_map/all_gather | solution.py:59
  100.7 35.8 %all_gather.31 = bf16[128,1024]{0,1:T(8,128)(2,1)S(1)} all-gather(bf16[128,32]{0,1:T(8,128)(2,1)} %param.20), channel_id=1, replica_groups=mesh['dp'=32,'mp'=8] {'dp'}, dimensions={1}, use_global_device_ids=true | all-gather | bytes 270336 | tf_op jit(solution)/shard_map/all_gather | solution.py:89
  136.6 1.7 convolution_convert_fusion.6
  138.5 1.7 convolution_convert_fusion.5
  141.6 1.7 convolution_convert_fusion.4
  143.8 1.4 fusion.3
  146.5 1.4 fusion.1
  149.3 1.4 convolution_convert_fusion
  152.0 62.7 %reduce-scatter.3.cloned.1.call-done = bf16[64,1024]{1,0:T(8,128)(2,1)} async-done(((bf16[512,1024]{1,0:T(8,128)(2,1)}), bf16[64,1024]{1,0:T(8,128)(2,1)}) %reduce-scatter.3.cloned.1.call-update) | async-done | bytes 131088 | tf_op jit(solution)/shard_map/reduce_scatter | solution.py:92
  215.8 1.1 multiply_reduce_fusion.1
  216.9 1.7 divide_convert_fusion.3
  218.8 70.8 %all-gather.13.cloned.1.call-done = bf16[1024,512]{1,0:T(8,128)(2,1)} async-done(((bf16[32,512]{1,0:T(8,128)(2,1)}), bf16[1024,512]{1,0:T(8,128)(2,1)}) %all-gather.13.cloned.1.call-update) | async-done | bytes 1048592 | tf_op jit(solution)/shard_map/all_gather | solution.py:98
  289.6 76.3 %all-gather.15.cloned.1.call-done = bf16[512,1024]{0,1:T(8,128)(2,1)} async-done(((bf16[512,32]{0,1:T(8,128)(2,1)}), bf16[512,1024]{0,1:T(8,128)(2,1)}) %all-gather.15.cloned.1.call-update) | async-done | bytes 1048592 | tf_op jit(solution)/shard_map/all_gather | solution.py:101
  365.9 30.5 %all-gather.11.cloned.1.call-done = bf16[512,1024]{1,0:T(8,128)(2,1)} async-done(((bf16[64,1024]{1,0:T(8,128)(2,1)}), bf16[512,1024]{1,0:T(8,128)(2,1)}) %all-gather.11.cloned.1.call-update) | async-done | bytes 1048592 | tf_op jit(solution)/shard_map/all_gather | solution.py:97
  396.4 6.2 %convolution_convert_fusion.1 = bf16[512,1024]{1,0:T(8,128)(2,1)} fusion(bf16[512,1024]{0,1:T(8,128)(2,1)} %all-gather.15.cloned.1.call-done, bf16[512,1024]{1,0:T(8,128)(2,1)} %all-gather.11.cloned.1.call-done, bf16[1024,512]{1,0:T(8,128)(2,1)} %all-gather.13.cloned.1.call-done), kind=kOutput, calls=%fused_computation.17 | convolution fusion | flops 1091305472 | bytes 4194304 | tf_op jit(solution)/shard_map/dot_general | solution.py:100
  402.9 1.1 gather_fusion
  406.2 9.6 %all-to-all-start.1 = ((s32[32,1,8]{2,1,0:T(1,128)}), s32[32,1,8]{2,1,0:T(1,128)S(1)}, u32[]{:S(2)}, u32[]{:S(2)}) async-start(s32[32,1,8]{2,1,0:T(1,128)} %bitcast.22), calls=%async_computation.3 | async-start | bytes 32768 | tf_op jit(solution)/shard_map/all_to_all | solution.py:135
  415.8 62.5 %all-gather = bf16[256,4,128]{2,1,0:T(4,128)(2,1)S(1)} all-gather(bf16[1,4,128]{2,1,0:T(4,128)(2,1)S(1)} %bitcast.99), channel_id=1, replica_groups=mesh['dp'=32,'mp'=8] {'dp','mp'}, dimensions={0}, use_global_device_ids=true | all-gather | bytes 263168 | tf_op jit(solution)/shard_map/all_gather | solution.py:108
  479.4 1.1 multiply_reduce_fusion
  480.5 1.3 multiply_reduce_fusion.2
  482.7 1.7 broadcast_in_dim.14
  484.3 13.7 %scatter_fusion = bf16[256,32,128]{2,1,0:T(8,128)(2,1)} fusion(bf16[256,32,128]{2,1,0:T(8,128)(2,1)} %broadcast_in_dim.14, s32[128]{0:T(128)S(1)} %fusion.75, bf16[128,32,128]{2,1,0:T(8,128)(2,1)S(1)} %gather_fusion.2), kind=kCustom, calls=%fused_computation.6 | custom fusion | bytes 3146240 | tf_op jit(solution)/shard_map/scatter | solution.py:132
  498.1 6.3 %all-to-all-start.2 = ((bf16[32,8,32,128]{3,2,1,0:T(8,128)(2,1)}), bf16[32,8,32,128]{3,2,1,0:T(8,128)(2,1)S(1)}, u32[]{:S(2)}, u32[]{:S(2)}) async-start(bf16[32,8,32,128]{3,2,1,0:T(8,128)(2,1)} %bitcast.25), calls=%async_computation.4 | async-start | bytes 4194304 | tf_op jit(solution)/shard_map/all_to_all | solution.py:140
  504.5 11.8 %gather_fusion.3 = bf16[256,128,128]{2,1,0:T(8,128)(2,1)} fusion(bf16[256,128,128]{2,1,0:T(8,128)(2,1)} %param.24, s32[1024]{0:T(1024)S(1)} %pad_clamp_fusion.2), kind=kCustom, calls=%fused_computation.3 | custom fusion | bytes 16778240 | tf_op jit(solution)/shard_map/gather | solution.py:136
  516.3 1.9 gather_fusion.1
  518.4 34.5 %all-to-all-done.2 = bf16[32,8,32,128]{3,2,1,0:T(8,128)(2,1)S(1)} async-done(((bf16[32,8,32,128]{3,2,1,0:T(8,128)(2,1)}), bf16[32,8,32,128]{3,2,1,0:T(8,128)(2,1)S(1)}, u32[]{:S(2)}, u32[]{:S(2)}) %all-to-all-start.2) | async-done | bytes 2097184 | tf_op jit(solution)/shard_map/all_to_all | solution.py:140
  552.9 8.0 %select_reduce_fusion = bf16[32,8,32]{2,1,0:T(8,128)(2,1)S(1)} fusion(bf16[32,8,32,128]{3,2,1,0:T(8,128)(2,1)S(1)} %all-to-all-done.2, bf16[32,8,128,128]{3,2,1,0:T(8,128)(2,1)} %bitcast.88, pred[32,8,128]{2,1,0:T(8,128)(4,1)S(1)} %iota_compare_fusion.1), kind=kOutput, calls=%fused_computation.8 | convolution fusion | flops 270524416 | bytes 10534912 | tf_op jit(solution)/shard_map/snie,snte->snit/dot_general | solution.py:138
  561.6 7.8 %all-to-all-start.3 = ((bf16[32,2,128]{2,1,0:T(2,128)(2,1)}), bf16[32,2,128]{2,1,0:T(2,128)(2,1)S(1)}, u32[]{:S(2)}, u32[]{:S(2)}) async-start(bf16[32,2,128]{2,1,0:T(2,128)(2,1)} %reshape.380), calls=%async_computation.5 | async-start | bytes 32768 | tf_op jit(solution)/shard_map/all_to_all | solution.py:28
  569.4 8.6 %all-to-all-done.3 = bf16[32,2,128]{2,1,0:T(2,128)(2,1)S(1)} async-done(((bf16[32,2,128]{2,1,0:T(2,128)(2,1)}), bf16[32,2,128]{2,1,0:T(2,128)(2,1)S(1)}, u32[]{:S(2)}, u32[]{:S(2)}) %all-to-all-start.3) | async-done | bytes 16416 | tf_op jit(solution)/shard_map/all_to_all | solution.py:28
  (88 shorter events, 15.4 us)
Async XLA Ops:
  7.2 395.7 %copy-start = (s32[8192]{0:T(1024)S(1)}, s32[8192]{0:T(1024)}, u32[]{:S(2)}) copy-start(s32[8192]{0:T(1024)} %param.26) | copy-start | bytes 98308
  7.2 129.4 %all-gather.7.cloned.1.call-start = ((), (), s32[]{:S(2)}) async-start(), calls=%async_computation.6 | async-start | bytes 1179648 | tf_op jit(solution)/shard_map/all_gather | solution.py:52
  7.9 133.7 %all-gather.9.cloned.1.call-start = ((), (), s32[]{:S(2)}) async-start(), calls=%async_computation.7 | async-start | bytes 1081344 | tf_op jit(solution)/shard_map/all_gather | solution.py:55
  10.1 128.4 %all-to-all-start = ((bf16[32,32,128]{2,1,0:T(8,128)(2,1)}), bf16[32,32,128]{2,1,0:T(8,128)(2,1)S(1)}, u32[]{:S(2)}, u32[]{:S(2)}) async-start(bf16[32,32,128]{2,1,0:T(8,128)(2,1)} %stack.2), calls=%async_computation | async-start | bytes 524288 | tf_op jit(solution)/shard_map/all_to_all | solution.py:12
  22.1 192.6 %reduce-scatter.3.cloned.1.call-start = ((), (), s32[]{:S(2)}) async-start(), calls=%async_computation.8 | async-start | bytes 1179648 | tf_op jit(solution)/shard_map/reduce_scatter | solution.py:92
  136.6 3.7 copy-start.3
  140.7 3.1 copy-start.8
  143.8 1.7 copy-start.4
  146.5 2.1 copy-start.7
  148.9 65.8 %copy-start.5 = (bf16[2,32,1024]{2,1,0:T(8,128)(2,1)S(1)}, bf16[2,32,1024]{2,1,0:T(8,128)(2,1)}, u32[]{:S(2)}) copy-start(bf16[2,32,1024]{2,1,0:T(8,128)(2,1)} %param.14) | copy-start | bytes 393220
  150.8 138.9 %all-gather.13.cloned.1.call-start = ((), (), s32[]{:S(2)}) async-start(), calls=%async_computation.10 | async-start | bytes 1081344 | tf_op jit(solution)/shard_map/all_gather | solution.py:98
  151.4 214.6 %all-gather.15.cloned.1.call-start = ((), (), s32[]{:S(2)}) async-start(), calls=%async_computation.11 | async-start | bytes 1081344 | tf_op jit(solution)/shard_map/all_gather | solution.py:101
  151.9 244.5 %all-gather.11.cloned.1.call-start = ((), (), s32[]{:S(2)}) async-start(), calls=%async_computation.9 | async-start | bytes 1179648 | tf_op jit(solution)/shard_map/all_gather | solution.py:97
  218.6 184.1 %copy-start.9 = (s32[2,16,4]{1,2,0:T(4,128)S(1)}, s32[2,16,4]{1,2,0:T(4,128)}, u32[]{:S(2)}) copy-start(s32[2,16,4]{1,2,0:T(4,128)} %param.27) | copy-start | bytes 1540
  218.6 197.2 %copy-start.10 = (bf16[4,128]{1,0:T(4,128)(2,1)S(1)}, bf16[4,128]{1,0:T(4,128)(2,1)}, u32[]{:S(2)}) copy-start(bf16[4,128]{1,0:T(4,128)(2,1)} %param.23) | copy-start | bytes 3076
  218.6 259.7 %reduce-scatter.5.cloned.1.call-start = ((), (), s32[]{:S(2)}) async-start(), calls=%async_computation.12 | async-start | bytes 1179648 | tf_op jit(solution)/shard_map/reduce_scatter | solution.py:103
  402.6 75.7 %copy-start.6 = (bf16[64,1024]{1,0:T(8,128)(2,1)S(1)}, bf16[64,1024]{1,0:T(8,128)(2,1)}, u32[]{:S(2)}) copy-start(bf16[64,1024]{1,0:T(8,128)(2,1)} %divide_convert_fusion.3) | copy-start | bytes 393220
  406.2 91.9 %all-to-all-start.1 = ((s32[32,1,8]{2,1,0:T(1,128)}), s32[32,1,8]{2,1,0:T(1,128)S(1)}, u32[]{:S(2)}, u32[]{:S(2)}) async-start(s32[32,1,8]{2,1,0:T(1,128)} %bitcast.22), calls=%async_computation.3 | async-start | bytes 32768 | tf_op jit(solution)/shard_map/all_to_all | solution.py:135
  481.9 2.5 copy-start.2
  498.1 54.9 %all-to-all-start.2 = ((bf16[32,8,32,128]{3,2,1,0:T(8,128)(2,1)}), bf16[32,8,32,128]{3,2,1,0:T(8,128)(2,1)S(1)}, u32[]{:S(2)}, u32[]{:S(2)}) async-start(bf16[32,8,32,128]{3,2,1,0:T(8,128)(2,1)} %bitcast.25), calls=%async_computation.4 | async-start | bytes 4194304 | tf_op jit(solution)/shard_map/all_to_all | solution.py:140
  504.4 11.8 %copy-start.1 = (s32[256]{0:T(256)S(1)}, s32[256]{0:T(256)}, u32[]{:S(2)}) copy-start(s32[256]{0:T(256)} %param.25) | copy-start | bytes 3076
  561.6 16.4 %all-to-all-start.3 = ((bf16[32,2,128]{2,1,0:T(2,128)(2,1)}), bf16[32,2,128]{2,1,0:T(2,128)(2,1)S(1)}, u32[]{:S(2)}, u32[]{:S(2)}) async-start(bf16[32,2,128]{2,1,0:T(2,128)(2,1)} %reshape.380), calls=%async_computation.5 | async-start | bytes 32768 | tf_op jit(solution)/shard_map/all_to_all | solution.py:28
Sparse Core Ops, SparseCore 0:
  9.8 29.9 all-gather.6
  42.4 71.3 all-gather.8
  150.9 63.7 reduce-scatter.2
  217.2 72.4 all-gather.12
  292.1 73.8 all-gather.14
  367.7 28.6 all-gather.10
  402.8 32.1 reduce-scatter.4
